TPU v7x, 128 devices: a whole 4x4x4 slice. The times are simulated.
128 devices in a mesh: seq: 16 (over z, x_lo, core), chan: 4 (over y), rep: 2 (over x_hi).
Axes of the slice: x: 4 (x_hi: 2, x_lo: 2; x = x_hi * 2 + x_lo), y: 4, z: 4, core: 2. Of those that a mesh axis runs over, the one named last changes fastest.
Arguments:
- inputs: bfloat16 [2, 4096, 2048], P('rep', 'seq', 'chan'), may hold values from -6 to 6
- w_in: bfloat16 [2048, 1536], P('chan'), may hold values from -0.25 to 0.25
- w_out: bfloat16 [2048, 2048], P('chan'), may hold values from -0.125 to 0.125
- filt_fwd: float32 [4096, 2048], P('seq', 'chan'), may hold values from -0.09375 to 0.09375
- filt_bwd: float32 [4096, 2048], P('seq', 'chan'), may hold values from -0.09375 to 0.09375
- skip_gain: float32 [2048], P('chan'), may hold values from -4 to 4
- cotangent: bfloat16 [2, 4096, 2048], P('rep', 'seq', 'chan'), may hold values from -6 to 6
Outputs:
- layer_out: bfloat16 [2, 4096, 2048], P('rep', 'seq', 'chan')
- d_input: bfloat16 [2, 4096, 2048], P('rep', 'seq', 'chan')
- d_w_in: float32 [2048, 1536], P('chan')
- d_w_out: float32 [2048, 2048], P('chan')
- d_filt_fwd: float32 [4096, 2048], P('seq', 'chan')
- d_filt_bwd: float32 [4096, 2048], P('seq', 'chan')
- d_skip: float32 [2048], P('chan')
All inputs are finite; a program needn't handle non-finite values.
Results may differ from a plain program's by a relative error of at most 0.005.
Values may be sent and summed in bfloat16 or wider, within the bound.
No kernel may reach another device: no remote copies, remote signals or barrier semaphores. Data moves between devices by JAX's collectives and lax.ppermute only.
A program may use at most 128 MiB of HBM per device.

v0:
```python
import math
import jax
import jax.numpy as jnp
from jax import lax
from jax.sharding import PartitionSpec as P

BLOCK = 512
HIGHEST_PRECISION = lax.Precision.HIGHEST


def wrapped_angle(phase, modulus, factor):
    centered = jnp.where(phase * 2 > modulus, phase - modulus, phase)
    return factor * math.pi / modulus * centered.astype(jnp.float32)


def unit_tables(table_size):
    index_row = jnp.arange(table_size, dtype=jnp.int32)
    phase = index_row[:, None] * index_row[None, :] % table_size
    angle = wrapped_angle(phase, table_size, 2.0)
    return (jnp.cos(angle), jnp.sin(angle))


def table_apply(table, fields, form):
    return jnp.einsum(form, table, fields, precision=HIGHEST_PRECISION)


def rotate(real_part, imag_part, angle):
    cosine = jnp.cos(angle)
    sine = jnp.sin(angle)
    return (real_part * cosine - imag_part * sine, real_part * sine + imag_part * cosine)


def complex_product(left_re, left_im, right_re, right_im):
    return (left_re * right_re - left_im * right_im, left_re * right_im + left_im * right_re)


def regroup(stacked):
    return lax.all_to_all(stacked, "seq", split_axis=1, concat_axis=1, tiled=True)


def forward_transform(fields):
    part_count = lax.axis_size("seq")
    position = lax.axis_index("seq")
    field_count, row_count, chan_width = fields.shape
    block_rows = row_count // part_count
    seq_length = row_count * part_count
    columns = regroup(fields).reshape(field_count, part_count, block_rows, chan_width)
    cos_part, sin_part = unit_tables(part_count)
    real_part = table_apply(cos_part, columns, "kp,fpbc->fkbc")
    imag_part = -table_apply(sin_part, columns, "kp,fpbc->fkbc")
    offsets = position * block_rows + jnp.arange(block_rows, dtype=jnp.int32)
    phase = jnp.arange(part_count, dtype=jnp.int32)[:, None] * offsets[None, :] % seq_length
    angle = wrapped_angle(phase, seq_length, -2.0)
    real_part, imag_part = rotate(real_part, imag_part, angle[None, :, :, None])
    merged = jnp.concatenate([real_part, imag_part], axis=0).reshape(
        2 * field_count, row_count, chan_width
    )
    spread = regroup(merged)
    real_part = spread[:field_count]
    imag_part = spread[field_count:]
    cos_rows, sin_rows = unit_tables(row_count)
    spec_re = table_apply(cos_rows, real_part, "kb,fbc->fkc") + table_apply(
        sin_rows, imag_part, "kb,fbc->fkc"
    )
    spec_im = table_apply(cos_rows, imag_part, "kb,fbc->fkc") - table_apply(
        sin_rows, real_part, "kb,fbc->fkc"
    )
    return (spec_re, spec_im)


def inverse_transform(spec_re, spec_im):
    part_count = lax.axis_size("seq")
    position = lax.axis_index("seq")
    field_count, row_count, chan_width = spec_re.shape
    block_rows = row_count // part_count
    seq_length = row_count * part_count
    cos_rows, sin_rows = unit_tables(row_count)
    time_re = table_apply(cos_rows, spec_re, "bk,fkc->fbc") - table_apply(
        sin_rows, spec_im, "bk,fkc->fbc"
    )
    time_im = table_apply(cos_rows, spec_im, "bk,fkc->fbc") + table_apply(
        sin_rows, spec_re, "bk,fkc->fbc"
    )
    phase = position * jnp.arange(row_count, dtype=jnp.int32) % seq_length
    angle = wrapped_angle(phase, seq_length, 2.0)
    time_re, time_im = rotate(time_re, time_im, angle[None, :, None])
    merged = jnp.concatenate([time_re, time_im], axis=0)
    spread = regroup(merged).reshape(2 * field_count, part_count, block_rows, chan_width)
    cos_part, sin_part = unit_tables(part_count)
    result = table_apply(cos_part, spread[:field_count], "pk,fkbc->fpbc") - table_apply(
        sin_part, spread[field_count:], "pk,fkbc->fpbc"
    )
    settled = regroup(result.reshape(field_count, row_count, chan_width))
    return settled * (1.0 / seq_length)


def on_device(inputs, w_in, w_out, filt_fwd, filt_bwd, skip_gain, cotangent):
    input_rows = inputs[0]
    row_count, chan_width = input_rows.shape
    block_count = chan_width // BLOCK
    input_blocks = input_rows.reshape(row_count, block_count, BLOCK)
    w_blocks = w_in.reshape(block_count, BLOCK, 3, BLOCK)
    projected = jnp.einsum(
        "mni,nisj->smnj", input_blocks, w_blocks, preferred_element_type=jnp.float32
    )
    projected = projected.reshape(3, row_count, chan_width)
    keys, values, queries = (projected[0], projected[1], projected[2])
    mixed = keys * values
    spec_re, spec_im = forward_transform(jnp.stack([mixed, filt_fwd, filt_bwd]))
    mix_re, mix_im = (spec_re[0], spec_im[0])
    fwd_re, fwd_im = (spec_re[1], spec_im[1])
    bwd_re, bwd_im = (spec_re[2], spec_im[2])
    joint_re, joint_im = complex_product(fwd_re + bwd_re, fwd_im - bwd_im, mix_re, mix_im)
    long_conv = inverse_transform(joint_re[None], joint_im[None])[0]
    conv_out = long_conv + skip_gain * mixed
    gated = (queries * conv_out).astype(jnp.bfloat16)
    out_terms = jnp.dot(gated, w_out, preferred_element_type=jnp.float32)
    layer_out = lax.psum_scatter(out_terms, "chan", scatter_dimension=1, tiled=True).astype(
        jnp.bfloat16
    )
    grad_rows = cotangent[0]
    piece = lax.all_gather(grad_rows, "chan", axis=1, tiled=True)
    grad_gated = lax.dot_general(
        piece, w_out, (((1,), (1,)), ((), ())), preferred_element_type=jnp.float32
    )
    block_grad = lax.dot_general(
        gated, piece, (((0,), (0,)), ((), ())), preferred_element_type=jnp.float32
    )
    grad_wout = block_grad
    grad_gated, grad_wout = (grad_gated, grad_wout)
    grad_queries = grad_gated * conv_out
    grad_conv = grad_gated * queries
    grad_re, grad_im = forward_transform(grad_conv[None])
    grad_re, grad_im = (grad_re[0], grad_im[0])
    upper_re, upper_im = complex_product(fwd_re + bwd_re, bwd_im - fwd_im, grad_re, grad_im)
    cross_re, cross_im = complex_product(grad_re, grad_im, mix_re, -mix_im)
    results = inverse_transform(
        jnp.stack([upper_re, cross_re, cross_re]), jnp.stack([upper_im, cross_im, -cross_im])
    )
    back = results[0]
    grad_hfwd = results[-2]
    grad_hbwd = results[-1]
    grad_mixed = back + skip_gain * grad_conv
    grad_pre = jnp.stack([grad_mixed * values, grad_mixed * keys, grad_queries]).astype(
        jnp.bfloat16
    )
    pre_blocks = grad_pre.reshape(3, row_count, block_count, BLOCK)
    d_input = jnp.einsum("smnj,nisj->mni", pre_blocks, w_blocks, preferred_element_type=jnp.float32)
    d_input = d_input.reshape(row_count, chan_width).astype(jnp.bfloat16)
    grad_win = jnp.einsum(
        "mni,smnj->nisj", input_blocks, pre_blocks, preferred_element_type=jnp.float32
    )
    grad_win = grad_win.reshape(chan_width, 3 * BLOCK)
    grad_skip = jnp.sum(grad_conv * mixed, axis=0)
    grad_win, grad_wout, grad_skip = lax.psum((grad_win, grad_wout, grad_skip), ("seq", "rep"))
    grad_hfwd, grad_hbwd = lax.psum((grad_hfwd, grad_hbwd), "rep")
    scale = 1.0 / math.sqrt(lax.axis_size("rep") * lax.axis_size("seq") * row_count)
    return (
        layer_out[None],
        d_input[None],
        grad_win * scale,
        grad_wout * scale,
        grad_hfwd * scale,
        grad_hbwd * scale,
        grad_skip * scale,
    )


def solution(mesh):
    return jax.shard_map(
        on_device,
        mesh=mesh,
        in_specs=(
            P("rep", "seq", "chan"),
            P("chan", None),
            P("chan", None),
            P("seq", "chan"),
            P("seq", "chan"),
            P("chan"),
            P("rep", "seq", "chan"),
        ),
        out_specs=(
            P("rep", "seq", "chan"),
            P("rep", "seq", "chan"),
            P("chan", None),
            P("chan", None),
            P("seq", "chan"),
            P("seq", "chan"),
            P("chan"),
        ),
        check_vma=False,
    )
```

profile of v0, /device:TPU:1, one launch (start us, length us, event | category | flops | bytes accessed | tf_op | source)
XLA Modules:
  0.0 551.9 jit_solution(10543586648825998175)
XLA Ops:
  10.6 3.2 fusion.67
  13.8 21.2 %all-gather.3.cloned.1.call-done = bf16[1,256,2048]{2,1,0:T(8,128)(2,1)} async-done(((bf16[1,256,512]{2,1,0:T(8,128)(2,1)}), bf16[1,256,2048]{2,1,0:T(8,128)(2,1)}) %all-gather.3.cloned.1.call-update) | async-done | bytes 1048592 | tf_op jit(solution)/shard_map/all_gather | solution.py:122
  34.9 3.2 multiply_reduce_fusion
  39.2 8.1 %all-to-all-start.4 = ((f32[1,256,512]{2,0,1:T(1,128)}), f32[1,256,512]{2,0,1:T(1,128)S(1)}, u32[]{:S(2)}, u32[]{:S(2)}) async-start(f32[1,256,512]{2,0,1:T(1,128)} %copy.104), calls=%async_computation.5 | async-start | bytes 1048576 | tf_op jit(solution)/shard_map/all_to_all | solution.py:38
  54.1 2.9 copy.85
  57.0 5.7 %all-to-all-start = ((f32[3,256,512]{2,0,1:T(4,128)}), f32[3,256,512]{2,0,1:T(4,128)}, u32[]{:S(2)}, u32[]{:S(2)}) async-start(f32[3,256,512]{2,0,1:T(4,128)} %copy.85), calls=%async_computation | async-start | bytes 4194304 | tf_op jit(solution)/shard_map/all_to_all | solution.py:38
  67.5 22.3 %all-to-all-done = f32[3,256,512]{2,0,1:T(4,128)} async-done(((f32[3,256,512]{2,0,1:T(4,128)}), f32[3,256,512]{2,0,1:T(4,128)}, u32[]{:S(2)}, u32[]{:S(2)}) %all-to-all-start) | async-done | bytes 1572896 | tf_op jit(solution)/shard_map/all_to_all | solution.py:38
  89.8 5.7 %all-to-all-start.5 = ((f32[2,256,512]{2,0,1:T(2,128)}), f32[2,256,512]{2,0,1:T(2,128)}, u32[]{:S(2)}, u32[]{:S(2)}) async-start(f32[2,256,512]{2,0,1:T(2,128)} %copy.110), calls=%async_computation.6 | async-start | bytes 2097152 | tf_op jit(solution)/shard_map/all_to_all | solution.py:38
  100.1 2.9 fusion
  105.4 3.9 copy.92
  111.2 5.6 %all-to-all-start.1 = ((f32[6,256,512]{2,0,1:T(8,128)}), f32[6,256,512]{2,0,1:T(8,128)}, u32[]{:S(2)}, u32[]{:S(2)}) async-start(f32[6,256,512]{2,0,1:T(8,128)} %copy.92), calls=%async_computation.1 | async-start | bytes 8388608 | tf_op jit(solution)/shard_map/all_to_all | solution.py:38
  125.7 40.5 %all-to-all-done.1 = f32[6,256,512]{2,0,1:T(8,128)} async-done(((f32[6,256,512]{2,0,1:T(8,128)}), f32[6,256,512]{2,0,1:T(8,128)}, u32[]{:S(2)}, u32[]{:S(2)}) %all-to-all-start.1) | async-done | bytes 3145760 | tf_op jit(solution)/shard_map/all_to_all | solution.py:38
  166.2 6.6 %fusion.279 = (f32[3,256,512]{2,0,1:T(4,128)}, f32[3,256,512]{2,0,1:T(4,128)}) fusion(f32[6,256,512]{2,0,1:T(8,128)} %all-to-all-done.1), kind=kLoop, calls=%fused_computation.333 | loop fusion | bytes 6291456 | tf_op jit(solution)/shard_map/slice | solution.py:59
  175.5 2.9 copy.134
  178.4 4.0 fusion.63
  189.9 3.8 fusion.277
  204.7 5.4 all-to-all-start.2
  210.1 3.9 fusion.11
  223.6 5.2 copy.111
  228.7 5.8 %all-to-all-start.6 = ((f32[6,256,512]{2,0,1:T(8,128)}), f32[6,256,512]{2,0,1:T(8,128)}, u32[]{:S(2)}, u32[]{:S(2)}) async-start(f32[6,256,512]{2,0,1:T(8,128)} %copy.111), calls=%async_computation.7 | async-start | bytes 8388608 | tf_op jit(solution)/shard_map/all_to_all | solution.py:38
  240.5 43.5 %all-to-all-done.6 = f32[6,256,512]{2,0,1:T(8,128)} async-done(((f32[6,256,512]{2,0,1:T(8,128)}), f32[6,256,512]{2,0,1:T(8,128)}, u32[]{:S(2)}, u32[]{:S(2)}) %all-to-all-start.6) | async-done | bytes 3145760 | tf_op jit(solution)/shard_map/all_to_all | solution.py:38
  284.0 4.6 all-to-all-start.3
  288.7 4.5 fusion.278
  302.6 5.8 %all-to-all-start.7 = ((f32[3,256,512]{2,0,1:T(4,128)}), f32[3,256,512]{2,0,1:T(4,128)}, u32[]{:S(2)}, u32[]{:S(2)}) async-start(f32[3,256,512]{2,0,1:T(4,128)} %copy.117), calls=%async_computation.8 | async-start | bytes 4194304 | tf_op jit(solution)/shard_map/all_to_all | solution.py:38
  309.6 25.8 %all-to-all-done.7 = f32[3,256,512]{2,0,1:T(4,128)} async-done(((f32[3,256,512]{2,0,1:T(4,128)}), f32[3,256,512]{2,0,1:T(4,128)}, u32[]{:S(2)}, u32[]{:S(2)}) %all-to-all-start.7) | async-done | bytes 1572896 | tf_op jit(solution)/shard_map/all_to_all | solution.py:38
  352.6 69.5 %psum.39 = f32[512]{0:T(512)S(1)} all-reduce(f32[512]{0:T(512)S(1)} %get-tuple-element.32), channel_id=1, replica_groups=mesh['seq'=16,'chan'=4,'rep'=2] {'seq','rep'}, use_global_device_ids=true, to_apply=%region_6.7 | all-reduce | flops 512 | bytes 4096 | tf_op jit(solution)/shard_map/psum | solution.py:155
  422.7 2.8 fusion.19
  428.7 82.8 %all-reduce.5.cloned.1.call-done = (f32[512,1536]{0,1:T(8,128)}, f32[512,2048]{1,0:T(8,128)}) async-done(((f32[512,1536]{0,1:T(8,128)}, f32[512,2048]{1,0:T(8,128)}), (f32[512,1536]{0,1:T(8,128)}, f32[512,2048]{1,0:T(8,128)})) %all-reduce.5.cloned.1.call-update) | async-done | bytes 7340048 | tf_op jit(solution)/shard_map/psum | solution.py:155
  511.6 3.9 broadcast_multiply_fusion.1
  515.5 3.5 copy.122
  519.0 5.0 broadcast_multiply_fusion
  524.0 19.1 %reduce-scatter.2.cloned.1.call-done = f32[256,512]{1,0:T(8,128)} async-done(((f32[256,2048]{1,0:T(8,128)}), f32[256,512]{1,0:T(8,128)}) %reduce-scatter.2.cloned.1.call-update) | async-done | bytes 524304 | tf_op jit(solution)/shard_map/reduce_scatter | solution.py:118
  (130 shorter events, 103.6 us)
Async XLA Ops:
  7.2 27.8 %copy-start = (bf16[512,2048]{1,0:T(8,128)(2,1)S(1)}, bf16[512,2048]{1,0:T(8,128)(2,1)}, u32[]{:S(2)}) copy-start(bf16[512,2048]{1,0:T(8,128)(2,1)} %param.9) | copy-start | bytes 6291460
  7.2 27.7 %all-gather.3.cloned.1.call-start = ((), (), s32[]{:S(2)}) async-start(), calls=%async_computation.10 | async-start | bytes 1310720 | tf_op jit(solution)/shard_map/all_gather | solution.py:122
  7.9 2.7 copy-start.19
  39.2 17.8 %all-to-all-start.4 = ((f32[1,256,512]{2,0,1:T(1,128)}), f32[1,256,512]{2,0,1:T(1,128)S(1)}, u32[]{:S(2)}, u32[]{:S(2)}) async-start(f32[1,256,512]{2,0,1:T(1,128)} %copy.104), calls=%async_computation.5 | async-start | bytes 1048576 | tf_op jit(solution)/shard_map/all_to_all | solution.py:38
  51.3 1.5 copy-start.6
  57.0 32.8 %all-to-all-start = ((f32[3,256,512]{2,0,1:T(4,128)}), f32[3,256,512]{2,0,1:T(4,128)}, u32[]{:S(2)}, u32[]{:S(2)}) async-start(f32[3,256,512]{2,0,1:T(4,128)} %copy.85), calls=%async_computation | async-start | bytes 4194304 | tf_op jit(solution)/shard_map/all_to_all | solution.py:38
  89.8 21.4 %all-to-all-start.5 = ((f32[2,256,512]{2,0,1:T(2,128)}), f32[2,256,512]{2,0,1:T(2,128)}, u32[]{:S(2)}, u32[]{:S(2)}) async-start(f32[2,256,512]{2,0,1:T(2,128)} %copy.110), calls=%async_computation.6 | async-start | bytes 2097152 | tf_op jit(solution)/shard_map/all_to_all | solution.py:38
  111.2 55.0 %all-to-all-start.1 = ((f32[6,256,512]{2,0,1:T(8,128)}), f32[6,256,512]{2,0,1:T(8,128)}, u32[]{:S(2)}, u32[]{:S(2)}) async-start(f32[6,256,512]{2,0,1:T(8,128)} %copy.92), calls=%async_computation.1 | async-start | bytes 8388608 | tf_op jit(solution)/shard_map/all_to_all | solution.py:38
  119.3 3.7 copy-start.11
  123.0 66.8 %copy-start.10 = (f32[1,256,512]{1,2,0:T(8,128)}, f32[1,256,512]{1,2,0:T(8,128)S(1)}, u32[]{:S(2)}) copy-start(f32[1,256,512]{1,2,0:T(8,128)S(1)} %fusion.15) | copy-start | bytes 1572868
  178.4 4.0 copy-start.1
  184.8 2.5 copy-start.2
  187.3 2.5 copy-start.12
  187.3 2.5 copy-start.22
  204.7 24.0 %all-to-all-start.2 = ((f32[2,256,512]{2,0,1:T(2,128)}), f32[2,256,512]{2,0,1:T(2,128)}, u32[]{:S(2)}, u32[]{:S(2)}) async-start(f32[2,256,512]{2,0,1:T(2,128)} %copy.95), calls=%async_computation.2 | async-start | bytes 2097152 | tf_op jit(solution)/shard_map/all_to_all | solution.py:38
  210.1 3.9 copy-start.8
  210.1 3.9 copy-start.9
  214.0 2.5 copy-start.13
  214.0 2.5 copy-start.14
  228.7 55.3 %all-to-all-start.6 = ((f32[6,256,512]{2,0,1:T(8,128)}), f32[6,256,512]{2,0,1:T(8,128)}, u32[]{:S(2)}, u32[]{:S(2)}) async-start(f32[6,256,512]{2,0,1:T(8,128)} %copy.111), calls=%async_computation.7 | async-start | bytes 8388608 | tf_op jit(solution)/shard_map/all_to_all | solution.py:38
  284.0 18.6 %all-to-all-start.3 = ((f32[1,256,512]{2,0,1:T(1,128)}), f32[1,256,512]{2,0,1:T(1,128)S(1)}, u32[]{:S(2)}, u32[]{:S(2)}) async-start(f32[1,256,512]{2,0,1:T(1,128)} %copy.101), calls=%async_computation.3 | async-start | bytes 1048576 | tf_op jit(solution)/shard_map/all_to_all | solution.py:38
  302.6 32.8 %all-to-all-start.7 = ((f32[3,256,512]{2,0,1:T(4,128)}), f32[3,256,512]{2,0,1:T(4,128)}, u32[]{:S(2)}, u32[]{:S(2)}) async-start(f32[3,256,512]{2,0,1:T(4,128)} %copy.117), calls=%async_computation.8 | async-start | bytes 4194304 | tf_op jit(solution)/shard_map/all_to_all | solution.py:38
  308.4 117.1 %all-reduce.7.cloned.1.call-start = ((), (), s32[]{:S(2)}) async-start(), calls=%async_computation.12 | async-start | bytes 2097152 | tf_op jit(solution)/shard_map/psum | solution.py:156
  341.9 169.6 %all-reduce.5.cloned.1.call-start = ((), (), s32[]{:S(2)}) async-start(), calls=%async_computation.11 | async-start | bytes 14680064 | tf_op jit(solution)/shard_map/psum | solution.py:155
  343.8 3.7 copy-start.15
  343.8 3.6 copy-start.17
  343.8 1.4 copy-start.20
  345.2 2.3 copy-start.4
  350.2 192.9 %reduce-scatter.2.cloned.1.call-start = ((), (), s32[]{:S(2)}) async-start(), calls=%async_computation.9 | async-start | bytes 2621440 | tf_op jit(solution)/shard_map/reduce_scatter | solution.py:118
  352.6 70.1 %copy-start.16 = (bf16[1,256,512]{1,2,0:T(8,128)(2,1)S(1)}, bf16[1,256,512]{1,2,0:T(8,128)(2,1)}, u32[]{:S(2)}) copy-start(bf16[1,256,512]{1,2,0:T(8,128)(2,1)} %copy-done.15) | copy-start | bytes 786436
  352.6 70.1 %copy-start.18 = (bf16[1,256,512]{1,2,0:T(8,128)(2,1)S(1)}, bf16[1,256,512]{1,2,0:T(8,128)(2,1)}, u32[]{:S(2)}) copy-start(bf16[1,256,512]{1,2,0:T(8,128)(2,1)} %copy-done.17) | copy-start | bytes 786436
  425.5 2.2 copy-start.21
  (4 other events, 4.9 us)
Sparse Core Ops, SparseCore 0:
  9.7 25.2 all-gather.2
  342.0 47.4 all-reduce.6
  393.7 117.8 all-reduce.4
  513.8 29.2 reduce-scatter.1
where the time goes:
time: 559 us; the launch traced here: 552 us
  waiting for transfers between devices  258 us (46%)
  matrix products  69.8 us (12%)
  blocking collectives  69.5 us (12%)
  local copies, waits for them, and re-layouts  68 us (12%)
  starting transfers between devices  47.1 us (8%)
  other arithmetic  24.7 us (4%)
  between operations  14.8 us (3%)
    all_to_all x8, waiting for transfers between devices, regroup(): lax.all_to_all(stacked, 'seq', split_axis=1, concat_axis=1, tiled=True)  134 us
    psum x1, waiting for transfers between devices, on_device(): lax.psum((grad_win, grad_wout, grad_skip), ('seq', 'rep'))  82.8 us
    psum x1, blocking collectives, on_device(): lax.psum((grad_win, grad_wout, grad_skip), ('seq', 'rep'))  69.5 us
    dot_general x24, matrix products, table_apply(): return jnp.einsum(form, table, fields, precision=HIGHEST_PRECISION)  53.6 us
    all_to_all x8, starting transfers between devices, regroup(): lax.all_to_all(stacked, 'seq', split_axis=1, concat_axis=1, tiled=True)  46.6 us
    all_gather x1, waiting for transfers between devices, on_device(): piece = lax.all_gather(grad_rows, 'chan', axis=1, tiled=True)  21.2 us
    unnamed x61, local copies, waits for them, and re-layouts  20.4 us
    reduce_scatter x1, waiting for transfers between devices, on_device(): lax.psum_scatter(out_terms, 'chan', scatter_dimension=1, tiled=True)  19.1 us
  transfers between devices with their start and end apart: 12, of which 8 were waited for; matrix products, arithmetic and copies ran while one was open for 20% of the time, Pallas kernels for 0%

commit v1 on v0

--- a/solution.py
+++ b/solution.py
@@ -6,6 +6,19 @@
 
 BLOCK = 512
 HIGHEST_PRECISION = lax.Precision.HIGHEST
+
+
+def gather_around(x, axis, dim):
+    ways = lax.axis_size(axis)
+    up = [(d, (d + 1) % ways) for d in range(ways)]
+    down = [(d, (d - 1) % ways) for d in range(ways)]
+    earlier, later = ([x], [x])
+    for _ in range(ways // 2):
+        earlier.append(lax.ppermute(earlier[-1], axis, up))
+    for _ in range((ways - 1) // 2):
+        later.append(lax.ppermute(later[-1], axis, down))
+    line = jnp.concatenate([*earlier[::-1], *later[1:]], axis=dim)
+    return jnp.roll(line, (lax.axis_index(axis) - ways // 2) * x.shape[dim], axis=dim)
 
 
 def wrapped_angle(phase, modulus, factor):
@@ -119,7 +132,7 @@
         jnp.bfloat16
     )
     grad_rows = cotangent[0]
-    piece = lax.all_gather(grad_rows, "chan", axis=1, tiled=True)
+    piece = gather_around(grad_rows, "chan", 1)
     grad_gated = lax.dot_general(
         piece, w_out, (((1,), (1,)), ((), ())), preferred_element_type=jnp.float32
     )

time: 559 us -> 530 us (0.948)
  waiting for transfers between devices: 258 us -> 224 us
    all_gather x1 -> x0, waiting for transfers between devices: 21.2 us -> none  [on_device(): piece = lax.all_gather(grad_rows, 'chan', axis=1, tiled=True)]
    reduce_scatter x1, waiting for transfers between devices: 19.1 us -> 0.01 us  [on_device(): lax.psum_scatter(out_terms, 'chan', scatter_dimension=1, tiled=True)]
    ppermute x0 -> x3, waiting for transfers between devices: none -> 9.05 us  [the longest x2 9.05 us: gather_around(): earlier.append(lax.ppermute(earlier[-1], axis, up))]
    unnamed x61 -> x74, local copies, waits for them, and re-layouts: 20.4 us -> 20.5 us
  transfers between devices with their start and end apart: 12 -> 14, of which waited for: 8 -> 8; matrix products, arithmetic and copies ran while one was open for 20% -> 21% of each run, Pallas kernels for 0% -> 0%
where the time goes in v1:
time: 530 us; the launch traced here: 522 us
  waiting for transfers between devices  224 us (42%)
  blocking collectives  70.1 us (13%)
  local copies, waits for them, and re-layouts  68.5 us (13%)
  matrix products  67.1 us (13%)
  starting transfers between devices  50.9 us (10%)
  other arithmetic  24.7 us (5%)
  between operations  16.6 us (3%)
    all_to_all x8, waiting for transfers between devices, regroup(): lax.all_to_all(stacked, 'seq', split_axis=1, concat_axis=1, tiled=True)  134 us
    psum x1, waiting for transfers between devices, on_device(): lax.psum((grad_win, grad_wout, grad_skip), ('seq', 'rep'))  80.9 us
    psum x1, blocking collectives, on_device(): lax.psum((grad_win, grad_wout, grad_skip), ('seq', 'rep'))  70.1 us
    dot_general x24, matrix products, table_apply(): return jnp.einsum(form, table, fields, precision=HIGHEST_PRECISION)  53.6 us
    all_to_all x8, starting transfers between devices, regroup(): lax.all_to_all(stacked, 'seq', split_axis=1, concat_axis=1, tiled=True)  46.9 us
    unnamed x74, local copies, waits for them, and re-layouts  20.5 us
  transfers between devices with their start and end apart: 14, of which 8 were waited for; matrix products, arithmetic and copies ran while one was open for 21% of the time, Pallas kernels for 0%

profile of v1, /device:TPU:1, one launch (start us, length us, event | category | flops | bytes accessed | tf_op | source)
XLA Modules:
  0.0 521.8 jit_solution(6308131110721262858)
XLA Ops:
  14.3 3.4 collective-permute-done
  19.8 5.6 %collective-permute-done.1 = bf16[256,512]{1,0:T(8,128)(2,1)S(1)} collective-permute-done((bf16[256,512]{1,0:T(8,128)(2,1)S(1)}, bf16[256,512]{1,0:T(8,128)(2,1)S(1)}, u32[]{:S(2)}, u32[]{:S(2)}) %collective-permute-start.1) | collective-permute-done | bytes 262176 | tf_op jit(solution)/shard_map/ppermute | solution.py:17
  28.5 8.3 %all-to-all-start.4 = ((f32[1,256,512]{2,0,1:T(1,128)}), f32[1,256,512]{2,0,1:T(1,128)S(1)}, u32[]{:S(2)}, u32[]{:S(2)}) async-start(f32[1,256,512]{2,0,1:T(1,128)} %copy.104), calls=%async_computation.5 | async-start | bytes 1048576 | tf_op jit(solution)/shard_map/all_to_all | solution.py:51
  43.6 2.9 copy.85
  46.5 5.7 %all-to-all-start = ((f32[3,256,512]{2,0,1:T(4,128)}), f32[3,256,512]{2,0,1:T(4,128)}, u32[]{:S(2)}, u32[]{:S(2)}) async-start(f32[3,256,512]{2,0,1:T(4,128)} %copy.85), calls=%async_computation | async-start | bytes 4194304 | tf_op jit(solution)/shard_map/all_to_all | solution.py:51
  57.0 22.3 %all-to-all-done = f32[3,256,512]{2,0,1:T(4,128)} async-done(((f32[3,256,512]{2,0,1:T(4,128)}), f32[3,256,512]{2,0,1:T(4,128)}, u32[]{:S(2)}, u32[]{:S(2)}) %all-to-all-start) | async-done | bytes 1572896 | tf_op jit(solution)/shard_map/all_to_all | solution.py:51
  79.3 5.7 %all-to-all-start.5 = ((f32[2,256,512]{2,0,1:T(2,128)}), f32[2,256,512]{2,0,1:T(2,128)}, u32[]{:S(2)}, u32[]{:S(2)}) async-start(f32[2,256,512]{2,0,1:T(2,128)} %copy.110), calls=%async_computation.6 | async-start | bytes 2097152 | tf_op jit(solution)/shard_map/all_to_all | solution.py:51
  89.6 2.9 fusion
  94.9 3.9 copy.92
  100.7 5.6 %all-to-all-start.1 = ((f32[6,256,512]{2,0,1:T(8,128)}), f32[6,256,512]{2,0,1:T(8,128)}, u32[]{:S(2)}, u32[]{:S(2)}) async-start(f32[6,256,512]{2,0,1:T(8,128)} %copy.92), calls=%async_computation.1 | async-start | bytes 8388608 | tf_op jit(solution)/shard_map/all_to_all | solution.py:51
  115.4 40.4 %all-to-all-done.1 = f32[6,256,512]{2,0,1:T(8,128)} async-done(((f32[6,256,512]{2,0,1:T(8,128)}), f32[6,256,512]{2,0,1:T(8,128)}, u32[]{:S(2)}, u32[]{:S(2)}) %all-to-all-start.1) | async-done | bytes 3145760 | tf_op jit(solution)/shard_map/all_to_all | solution.py:51
  155.8 6.6 %fusion.281 = (f32[3,256,512]{2,0,1:T(4,128)}, f32[3,256,512]{2,0,1:T(4,128)}) fusion(f32[6,256,512]{2,0,1:T(8,128)} %all-to-all-done.1), kind=kLoop, calls=%fused_computation.343 | loop fusion | bytes 6291456 | tf_op jit(solution)/shard_map/slice | solution.py:72
  165.0 2.9 copy.134
  167.9 4.0 fusion.63
  179.4 3.8 fusion.279
  194.2 5.3 %all-to-all-start.2 = ((f32[2,256,512]{2,0,1:T(2,128)}), f32[2,256,512]{2,0,1:T(2,128)}, u32[]{:S(2)}, u32[]{:S(2)}) async-start(f32[2,256,512]{2,0,1:T(2,128)} %copy.95), calls=%async_computation.2 | async-start | bytes 2097152 | tf_op jit(solution)/shard_map/all_to_all | solution.py:51
  199.6 3.9 fusion.11
  208.5 2.7 subtract_bitcast_fusion.1
  213.1 5.2 copy.111
  218.2 5.8 %all-to-all-start.6 = ((f32[6,256,512]{2,0,1:T(8,128)}), f32[6,256,512]{2,0,1:T(8,128)}, u32[]{:S(2)}, u32[]{:S(2)}) async-start(f32[6,256,512]{2,0,1:T(8,128)} %copy.111), calls=%async_computation.7 | async-start | bytes 8388608 | tf_op jit(solution)/shard_map/all_to_all | solution.py:51
  230.2 43.4 %all-to-all-done.6 = f32[6,256,512]{2,0,1:T(8,128)} async-done(((f32[6,256,512]{2,0,1:T(8,128)}), f32[6,256,512]{2,0,1:T(8,128)}, u32[]{:S(2)}, u32[]{:S(2)}) %all-to-all-start.6) | async-done | bytes 3145760 | tf_op jit(solution)/shard_map/all_to_all | solution.py:51
  273.5 4.6 all-to-all-start.3
  278.2 4.5 fusion.280
  292.1 5.8 %all-to-all-start.7 = ((f32[3,256,512]{2,0,1:T(4,128)}), f32[3,256,512]{2,0,1:T(4,128)}, u32[]{:S(2)}, u32[]{:S(2)}) async-start(f32[3,256,512]{2,0,1:T(4,128)} %copy.117), calls=%async_computation.8 | async-start | bytes 4194304 | tf_op jit(solution)/shard_map/all_to_all | solution.py:51
  299.1 25.8 %all-to-all-done.7 = f32[3,256,512]{2,0,1:T(4,128)} async-done(((f32[3,256,512]{2,0,1:T(4,128)}), f32[3,256,512]{2,0,1:T(4,128)}, u32[]{:S(2)}, u32[]{:S(2)}) %all-to-all-start.7) | async-done | bytes 1572896 | tf_op jit(solution)/shard_map/all_to_all | solution.py:51
  336.9 2.7 fusion.21
  342.1 70.1 %psum.39 = f32[512]{0:T(512)S(1)} all-reduce(f32[512]{0:T(512)S(1)} %get-tuple-element.32), channel_id=1, replica_groups=mesh['seq'=16,'chan'=4,'rep'=2] {'seq','rep'}, use_global_device_ids=true, to_apply=%region_6.7 | all-reduce | flops 512 | bytes 4096 | tf_op jit(solution)/shard_map/psum | solution.py:168
  412.8 2.7 fusion.19
  418.7 80.9 %all-reduce.5.cloned.1.call-done = (f32[512,1536]{0,1:T(8,128)}, f32[512,2048]{1,0:T(8,128)}) async-done(((f32[512,1536]{0,1:T(8,128)}, f32[512,2048]{1,0:T(8,128)}), (f32[512,1536]{0,1:T(8,128)}, f32[512,2048]{1,0:T(8,128)})) %all-reduce.5.cloned.1.call-update) | async-done | bytes 7340048 | tf_op jit(solution)/shard_map/psum | solution.py:168
  499.7 3.9 broadcast_multiply_fusion.1
  503.6 3.5 copy.122
  507.1 5.0 broadcast_multiply_fusion
  (147 shorter events, 105.3 us)
Async XLA Ops:
  8.0 17.8 %copy-start = (bf16[512,2048]{1,0:T(8,128)(2,1)S(1)}, bf16[512,2048]{1,0:T(8,128)(2,1)}, u32[]{:S(2)}) copy-start(bf16[512,2048]{1,0:T(8,128)(2,1)} %param.9) | copy-start | bytes 6291460
  8.0 9.7 %collective-permute-start = (bf16[256,512]{1,0:T(8,128)(2,1)}, bf16[256,512]{1,0:T(8,128)(2,1)S(1)}, u32[]{:S(2)}, u32[]{:S(2)}) collective-permute-start(bf16[256,512]{1,0:T(8,128)(2,1)} %bitcast.270), channel_id=1, source_target_pairs={{0,2},{2,4},{4,6},{6,0},{1,3},{3,5},{5,7},{7,1},{8,10},{10,12},{12... | collective-permute-start | bytes 786440 | tf_op jit(solution)/shard_map/ppermute | solution.py:17
  10.2 15.4 %collective-permute-start.2 = (bf16[256,512]{1,0:T(8,128)(2,1)}, bf16[256,512]{1,0:T(8,128)(2,1)S(1)}, u32[]{:S(2)}, u32[]{:S(2)}) collective-permute-start(bf16[256,512]{1,0:T(8,128)(2,1)} %bitcast.271), channel_id=1, source_target_pairs={{0,6},{2,0},{4,2},{6,4},{1,7},{3,1},{5,3},{7,5},{8,14},{10,8},{12,... | collective-permute-start | bytes 786440 | tf_op jit(solution)/shard_map/ppermute | solution.py:19
  11.7 6.0 %copy-start.22 = (bf16[1,256,512]{2,1,0:T(8,128)(2,1)S(1)}, bf16[1,256,512]{2,1,0:T(8,128)(2,1)}, u32[]{:S(2)}) copy-start(bf16[1,256,512]{2,1,0:T(8,128)(2,1)} %param.7) | copy-start | bytes 786436
  17.8 7.7 %collective-permute-start.1 = (bf16[256,512]{1,0:T(8,128)(2,1)S(1)}, bf16[256,512]{1,0:T(8,128)(2,1)S(1)}, u32[]{:S(2)}, u32[]{:S(2)}) collective-permute-start(bf16[256,512]{1,0:T(8,128)(2,1)S(1)} %collective-permute-done), channel_id=1, source_target_pairs={{0,2},{2,4},{4,6},{6,0},{1,3},{3,5},{5,7},{7,1},{8,10},{10,12},{12... | collective-permute-start | bytes 786440 | tf_op jit(solution)/shard_map/ppermute | solution.py:17
  17.8 7.8 %copy-start.17 = (bf16[1,256,512]{2,1,0:T(8,128)(2,1)S(1)}, bf16[1,256,512]{2,1,0:T(8,128)(2,1)}, u32[]{:S(2)}) copy-start(bf16[1,256,512]{2,1,0:T(8,128)(2,1)} %param.13) | copy-start | bytes 786436
  19.8 5.9 %copy-start.1 = (f32[3,512,256]{2,1,0:T(8,128)}, f32[3,512,256]{2,1,0:T(8,128)S(1)}, u32[]{:S(2)}) copy-start(f32[3,512,256]{2,1,0:T(8,128)S(1)} %fusion.67) | copy-start | bytes 4718596
  28.5 18.1 %all-to-all-start.4 = ((f32[1,256,512]{2,0,1:T(1,128)}), f32[1,256,512]{2,0,1:T(1,128)S(1)}, u32[]{:S(2)}, u32[]{:S(2)}) async-start(f32[1,256,512]{2,0,1:T(1,128)} %copy.104), calls=%async_computation.5 | async-start | bytes 1048576 | tf_op jit(solution)/shard_map/all_to_all | solution.py:51
  46.5 32.8 %all-to-all-start = ((f32[3,256,512]{2,0,1:T(4,128)}), f32[3,256,512]{2,0,1:T(4,128)}, u32[]{:S(2)}, u32[]{:S(2)}) async-start(f32[3,256,512]{2,0,1:T(4,128)} %copy.85), calls=%async_computation | async-start | bytes 4194304 | tf_op jit(solution)/shard_map/all_to_all | solution.py:51
  79.3 21.4 %all-to-all-start.5 = ((f32[2,256,512]{2,0,1:T(2,128)}), f32[2,256,512]{2,0,1:T(2,128)}, u32[]{:S(2)}, u32[]{:S(2)}) async-start(f32[2,256,512]{2,0,1:T(2,128)} %copy.110), calls=%async_computation.6 | async-start | bytes 2097152 | tf_op jit(solution)/shard_map/all_to_all | solution.py:51
  100.7 55.0 %all-to-all-start.1 = ((f32[6,256,512]{2,0,1:T(8,128)}), f32[6,256,512]{2,0,1:T(8,128)}, u32[]{:S(2)}, u32[]{:S(2)}) async-start(f32[6,256,512]{2,0,1:T(8,128)} %copy.92), calls=%async_computation.1 | async-start | bytes 8388608 | tf_op jit(solution)/shard_map/all_to_all | solution.py:51
  109.0 3.7 copy-start.13
  112.7 66.7 %copy-start.12 = (f32[1,256,512]{1,2,0:T(8,128)}, f32[1,256,512]{1,2,0:T(8,128)S(1)}, u32[]{:S(2)}) copy-start(f32[1,256,512]{1,2,0:T(8,128)S(1)} %fusion.15) | copy-start | bytes 1572868
  167.9 4.0 copy-start.2
  174.3 2.5 copy-start.3
  176.8 2.5 copy-start.14
  176.9 2.5 copy-start.25
  194.2 24.0 %all-to-all-start.2 = ((f32[2,256,512]{2,0,1:T(2,128)}), f32[2,256,512]{2,0,1:T(2,128)}, u32[]{:S(2)}, u32[]{:S(2)}) async-start(f32[2,256,512]{2,0,1:T(2,128)} %copy.95), calls=%async_computation.2 | async-start | bytes 2097152 | tf_op jit(solution)/shard_map/all_to_all | solution.py:51
  199.6 3.9 copy-start.10
  199.6 3.9 copy-start.11
  203.5 2.5 copy-start.15
  203.5 2.5 copy-start.16
  218.2 55.3 %all-to-all-start.6 = ((f32[6,256,512]{2,0,1:T(8,128)}), f32[6,256,512]{2,0,1:T(8,128)}, u32[]{:S(2)}, u32[]{:S(2)}) async-start(f32[6,256,512]{2,0,1:T(8,128)} %copy.111), calls=%async_computation.7 | async-start | bytes 8388608 | tf_op jit(solution)/shard_map/all_to_all | solution.py:51
  273.5 18.6 %all-to-all-start.3 = ((f32[1,256,512]{2,0,1:T(1,128)}), f32[1,256,512]{2,0,1:T(1,128)S(1)}, u32[]{:S(2)}, u32[]{:S(2)}) async-start(f32[1,256,512]{2,0,1:T(1,128)} %copy.101), calls=%async_computation.3 | async-start | bytes 1048576 | tf_op jit(solution)/shard_map/all_to_all | solution.py:51
  292.1 32.8 %all-to-all-start.7 = ((f32[3,256,512]{2,0,1:T(4,128)}), f32[3,256,512]{2,0,1:T(4,128)}, u32[]{:S(2)}, u32[]{:S(2)}) async-start(f32[3,256,512]{2,0,1:T(4,128)} %copy.117), calls=%async_computation.8 | async-start | bytes 4194304 | tf_op jit(solution)/shard_map/all_to_all | solution.py:51
  297.9 117.6 %all-reduce.7.cloned.1.call-start = ((), (), s32[]{:S(2)}) async-start(), calls=%async_computation.11 | async-start | bytes 2097152 | tf_op jit(solution)/shard_map/psum | solution.py:169
  331.4 168.2 %all-reduce.5.cloned.1.call-start = ((), (), s32[]{:S(2)}) async-start(), calls=%async_computation.10 | async-start | bytes 14680064 | tf_op jit(solution)/shard_map/psum | solution.py:168
  333.3 3.7 copy-start.18
  333.3 3.6 copy-start.20
  339.7 172.4 %reduce-scatter.2.cloned.1.call-start = ((), (), s32[]{:S(2)}) async-start(), calls=%async_computation.9 | async-start | bytes 2621440 | tf_op jit(solution)/shard_map/reduce_scatter | solution.py:131
  342.1 70.7 %copy-start.19 = (bf16[1,256,512]{1,2,0:T(8,128)(2,1)S(1)}, bf16[1,256,512]{1,2,0:T(8,128)(2,1)}, u32[]{:S(2)}) copy-start(bf16[1,256,512]{1,2,0:T(8,128)(2,1)} %copy-done.18) | copy-start | bytes 786436
  342.1 70.7 %copy-start.21 = (bf16[1,256,512]{1,2,0:T(8,128)(2,1)S(1)}, bf16[1,256,512]{1,2,0:T(8,128)(2,1)}, u32[]{:S(2)}) copy-start(bf16[1,256,512]{1,2,0:T(8,128)(2,1)} %copy-done.20) | copy-start | bytes 786436
  (9 other events, 13.9 us)
Sparse Core Ops, SparseCore 0:
  331.5 46.0 all-reduce.6
  381.7 117.8 all-reduce.4
Sparse Core Ops, SparseCore 1:
  342.6 26.8 reduce-scatter.1
